TPU v7x, 256 devices: a whole 4x4x8 slice. The times are simulated.
256 devices in a mesh: dp: 8 (over z), seq: 32 (over y, x, core).
Axes of the slice: x: 4, y: 4, z: 8, core: 2. Of those that a mesh axis runs over, the one named last changes fastest.
Arguments:
- inputs: bfloat16 [8, 4096, 2048], P('dp', 'seq'), may hold values from -6 to 6
- weight_codes: bfloat16 [2048, 1280], P('seq'), may hold values from -4 to 4
- scales: bfloat16 [2048, 10], P('seq'), may hold values from 0.010986328 to 0.043945312
- log_decay: float32 [8, 16, 4096], P('dp', None, 'seq'), may hold values from -0.85 to 0, as said below
- cotangent: bfloat16 [8, 4096, 1024], P('dp', 'seq'), may hold values from -6 to 6
Outputs:
- grad_inputs: float32 [8, 4096, 2048], P('dp', 'seq')
- grad_weight: float32 [2048, 1280], P('seq')
Inputs may be any that keep to these rules, and one draw needn't show every extreme that they name: log_decay is negative everywhere.
All inputs are finite; a program needn't handle non-finite values.
Results may differ from a plain program's by a relative error of at most 0.017.
Values may be sent and summed in bfloat16 or wider, within the bound.
No kernel may reach another device: no remote copies, remote signals or barrier semaphores. Data moves between devices by JAX's collectives and lax.ppermute only.
A program may use at most 128 MiB of HBM per device.

v0:
```python
import math
import jax
import jax.numpy as jnp
from jax import lax
from jax.sharding import PartitionSpec as P


def entering(part, axis, combine, identity, reverse):
    count = lax.axis_size(axis)
    place = lax.axis_index(axis)
    ahead = count - 1 - place if reverse else place
    gathered = jax.tree.map(lambda a: lax.all_gather(a, axis), part)
    state = jax.tree.map(lambda a, e: jnp.zeros_like(a) + jnp.asarray(e, a.dtype), part, identity)

    def one(hop, state):
        source = count - 1 - hop if reverse else hop
        return combine(
            state, jax.tree.map(lambda a: lax.dynamic_index_in_dim(a, source, 0, False), gathered)
        )

    return lax.fori_loop(0, ahead, one, state)


def dequantize(code_rows, scale_rows):
    row_count, col_count = code_rows.shape
    group_count = scale_rows.shape[1]
    spread = code_rows.astype(jnp.float32).reshape(row_count, group_count, col_count // group_count)
    spread = spread * scale_rows.astype(jnp.float32)[:, :, None]
    return spread.reshape(row_count, col_count).astype(jnp.bfloat16)


def block_prep(ld_block):
    cum_log = jnp.cumsum(ld_block, axis=1)
    input_scale = jnp.sqrt(-jnp.expm1(2.0 * ld_block))
    tail_weight = jnp.exp(cum_log[:, -1:] - cum_log) * input_scale
    return (cum_log, input_scale, tail_weight)


def weighted_pair(x_vals, grad_out, tail_weight, cum_log, inv_root):
    head_weight = jnp.exp(cum_log) * inv_root
    weighted_x = (x_vals.astype(jnp.float32) * tail_weight.T[:, :, None]).astype(jnp.bfloat16)
    weighted_g = (grad_out.astype(jnp.float32) * head_weight.T[:, :, None]).astype(jnp.bfloat16)
    return (weighted_x, weighted_g)


def summaries(x_vals, b_mat, c_mat, grad_out, ld_block):
    cum_log, input_scale, tail_weight = block_prep(ld_block)
    inv_root = 1.0 / math.sqrt(b_mat.shape[1])
    weighted_x, weighted_g = weighted_pair(x_vals, grad_out, tail_weight, cum_log, inv_root)
    fwd_state = jnp.einsum("sn,shp->hnp", b_mat, weighted_x, preferred_element_type=jnp.float32)
    back_state = jnp.einsum("tn,thp->hnp", c_mat, weighted_g, preferred_element_type=jnp.float32)
    return (jnp.exp(cum_log[:, -1]), fwd_state, back_state)


def block_grads(x_vals, b_mat, c_mat, grad_out, ld_block, state_in, back_in):
    block_len = ld_block.shape[1]
    cum_log, input_scale, tail_weight = block_prep(ld_block)
    inv_root = 1.0 / math.sqrt(b_mat.shape[1])
    weighted_x, weighted_g = weighted_pair(x_vals, grad_out, tail_weight, cum_log, inv_root)
    row_ids = lax.broadcasted_iota(jnp.int32, (block_len, block_len), 0)
    col_ids = lax.broadcasted_iota(jnp.int32, (block_len, block_len), 1)
    lower_mask = (row_ids >= col_ids)[None]
    log_gap = cum_log[:, :, None] - cum_log[:, None, :]
    decay_mat = jnp.where(lower_mask, jnp.exp(jnp.where(lower_mask, log_gap, 0.0)), 0.0)
    state_low = state_in.astype(jnp.bfloat16)
    back_low = back_in.astype(jnp.bfloat16)
    x_dot_g = jnp.einsum("thp,shp->hts", grad_out, x_vals, preferred_element_type=jnp.float32)
    c_dot_b = jnp.dot(c_mat, b_mat.T, preferred_element_type=jnp.float32)
    mix_weights = (
        jnp.sum(decay_mat * input_scale[:, None, :] * x_dot_g, axis=0) * inv_root
    ).astype(jnp.bfloat16)
    d_c = jnp.einsum("hnp,thp->tn", state_low, weighted_g, preferred_element_type=jnp.float32)
    d_c = d_c + jnp.dot(mix_weights, b_mat, preferred_element_type=jnp.float32)
    d_b = jnp.einsum("hnp,thp->tn", back_low, weighted_x, preferred_element_type=jnp.float32)
    d_b = d_b + jnp.dot(mix_weights.T, c_mat, preferred_element_type=jnp.float32)
    d_x = (
        jnp.einsum("tn,hnp->thp", b_mat, back_low, preferred_element_type=jnp.float32)
        * tail_weight.T[:, :, None]
    )
    inner_weights = (decay_mat * c_dot_b[None] * inv_root).astype(jnp.bfloat16)
    inner = jnp.einsum("hus,uhp->shp", inner_weights, grad_out, preferred_element_type=jnp.float32)
    d_x = d_x + input_scale.T[:, :, None] * inner
    return (d_x, d_b, d_c)


def state_chain(decays, adds, start, backward):

    def step(carry, item):
        return (item[0][:, None, None] * carry + item[1], carry)

    return lax.scan(step, start, (decays, adds), reverse=backward)


def join_summary(earlier, later):
    return (earlier[0] * later[0], later[0][:, None, None] * earlier[1] + later[1])


def local(inputs, weight_codes, scales, log_decay, cotangent):
    tok_count = inputs.shape[1]
    features = inputs[0]
    grad_out = cotangent[0]
    head_count = log_decay.shape[1]
    hp_width = grad_out.shape[1]
    head_dim = hp_width // head_count
    proj_width = weight_codes.shape[1]
    state_width = (proj_width - hp_width) // 2
    full_codes, full_scales = (
        lax.all_gather(weight_codes, "seq", axis=0, tiled=True),
        lax.all_gather(scales, "seq", axis=0, tiled=True),
    )
    weights = dequantize(full_codes, full_scales)
    projected = jnp.dot(features, weights, preferred_element_type=jnp.float32).astype(jnp.bfloat16)
    block_len = min(128, tok_count)
    block_count = tok_count // block_len
    x_blocks = projected[:, :hp_width].reshape(block_count, block_len, head_count, head_dim)
    b_blocks = projected[:, hp_width : hp_width + state_width].reshape(
        block_count, block_len, state_width
    )
    c_blocks = projected[:, hp_width + state_width :].reshape(block_count, block_len, state_width)
    g_blocks = grad_out.reshape(block_count, block_len, head_count, head_dim)
    ld_blocks = log_decay[0].reshape(head_count, block_count, block_len).transpose(1, 0, 2)
    decays, fwd_states, back_states = jax.vmap(summaries)(
        x_blocks, b_blocks, c_blocks, g_blocks, ld_blocks
    )
    zero_state = jnp.zeros((head_count, state_width, head_dim), jnp.float32)
    dev_decay = jnp.prod(decays, axis=0)
    dev_fwd, unused_a = state_chain(decays, fwd_states, zero_state, False)
    dev_back, unused_b = state_chain(decays, back_states, zero_state, True)
    neutral = (jnp.ones((head_count,), jnp.float32), zero_state)
    carried = entering((dev_decay, dev_fwd), "seq", join_summary, neutral, False)
    returned = entering((dev_decay, dev_back), "seq", join_summary, neutral, True)
    unused_c, state_starts = state_chain(decays, fwd_states, carried[1], False)
    unused_d, back_starts = state_chain(decays, back_states, returned[1], True)
    d_x, d_b, d_c = lax.map(
        lambda block_item: block_grads(*block_item),
        (x_blocks, b_blocks, c_blocks, g_blocks, ld_blocks, state_starts, back_starts),
    )
    d_proj = jnp.concatenate(
        [
            d_x.reshape(tok_count, hp_width),
            d_b.reshape(tok_count, state_width),
            d_c.reshape(tok_count, state_width),
        ],
        axis=1,
    ).astype(jnp.bfloat16)
    grad_in = lax.dot_general(
        d_proj, weights, (((1,), (1,)), ((), ())), preferred_element_type=jnp.float32
    )
    seq_count = lax.axis_size("seq")
    group_count = lax.axis_size("dp")
    norm_factor = 1.0 / math.sqrt(group_count * seq_count * tok_count)
    partial_grad = lax.psum_scatter(
        lax.dot_general(
            features, d_proj, (((0,), (0,)), ((), ())), preferred_element_type=jnp.float32
        ),
        "seq",
        scatter_dimension=0,
        tiled=True,
    )
    summed_grad = lax.psum(partial_grad, "dp")
    return (grad_in[None], summed_grad * norm_factor)


def solution(mesh):
    placed = (
        P("dp", "seq", None),
        P("seq", None),
        P("seq", None),
        P("dp", None, "seq"),
        P("dp", "seq", None),
    )
    return jax.shard_map(
        local,
        mesh=mesh,
        in_specs=placed,
        out_specs=(P("dp", "seq", None), P("seq", None)),
        check_vma=False,
    )
```

profile of v0, /device:TPU:2, one launch (start us, length us, event | category | flops | bytes accessed | tf_op | source)
XLA Modules:
  0.0 521.6 jit_solution(17085878530613788069)
XLA Ops:
  8.0 24.6 %all-gather.1 = bf16[32,64,10]{1,2,0:T(8,128)(2,1)S(1)} all-gather(bf16[1,64,10]{1,2,0:T(8,128)(2,1)} %bitcast.145), channel_id=1, replica_groups=mesh['dp'=8,'seq'=32] {'seq'}, dimensions={0}, use_global_device_ids=true | all-gather | bytes 42240 | tf_op jit(solution)/shard_map/all_gather | solution.py:109
  35.8 1.3 fusion.43
  37.1 28.6 %all-gather.6.cloned.1.call-done = bf16[2048,1280]{1,0:T(8,128)(2,1)} async-done(((bf16[64,1280]{1,0:T(8,128)(2,1)}), bf16[2048,1280]{1,0:T(8,128)(2,1)}) %all-gather.6.cloned.1.call-update) | async-done | bytes 5242896 | tf_op jit(solution)/shard_map/all_gather | solution.py:108
  65.7 7.9 %copy.59 = bf16[2048,1280]{0,1:T(8,128)(2,1)} copy(bf16[2048,1280]{1,0:T(8,128)(2,1)} %all-gather.6.cloned.1.call-done) | data formatting | bytes 10485760 | tf_op jit(solution)/shard_map/all_gather | solution.py:108
  73.6 3.9 fusion
  77.6 2.4 copy-done.2
  80.0 1.5 fusion.1
  85.5 21.4 %all-gather = f32[32,16,1]{1,2,0:T(1,128)} all-gather(f32[1,16,1]{1,2,0:T(1,128)S(1)} %exp.58), channel_id=2, replica_groups=mesh['dp'=8,'seq'=32] {'seq'}, dimensions={0}, use_global_device_ids=true | all-gather | bytes 2112 | tf_op jit(solution)/shard_map/all_gather | solution.py:12
  108.7 52.1 %all-gather.10.cloned.1.call-done = f32[32,16,128,64]{2,3,1,0:T(8,128)} async-done(((f32[1,16,128,64]{2,3,1,0:T(8,128)}), f32[32,16,128,64]{2,3,1,0:T(8,128)}) %all-gather.10.cloned.1.call-update) | async-done | bytes 16777232 | tf_op jit(solution)/shard_map/all_gather | solution.py:12
  160.9 4.7 while.17
  160.9 1.1 constant_dynamic-slice_fusion.5
  163.3 1.1 constant_dynamic-slice_fusion.5
  165.6 74.8 %all-gather.8.cloned.1.call-done = f32[32,16,128,64]{2,3,1,0:T(8,128)} async-done(((f32[1,16,128,64]{2,3,1,0:T(8,128)}), f32[32,16,128,64]{2,3,1,0:T(8,128)}) %all-gather.8.cloned.1.call-update) | async-done | bytes 16777232 | tf_op jit(solution)/shard_map/all_gather | solution.py:12
  240.5 68.7 %while.16 = (s32[]{:T(128)}, f32[16,128,64]{2,1,0:T(8,128)S(1)}, s32[]{:T(128)}, f32[32,16]{1,0:T(8,128)}, f32[32,16,128,64]{2,3,1,0:T(8,128)}, /*index=5*/s32[]{:T(128)}, s32[]{:T(128)}, s32[]{:T(128)}, s32[]{:T(128)}) while((s32[]{:T(128)}, f32[16,128,64]{2,1,0:T(8,128)S(1)}, s32[]{:T(128)}, f32[32,16]{1,0:T(8,128)}, ...), condition=%wide.region_2.3_spmd, body=%wide.region_1.2_spmd.sunk | while | flops 262150 | bytes 3670363 | solution.py:21
  245.3 1.1 constant_dynamic-slice_fusion.4
  247.7 1.1 constant_dynamic-slice_fusion.4
  250.1 1.1 constant_dynamic-slice_fusion.4
  252.4 1.1 constant_dynamic-slice_fusion.4
  254.8 1.1 constant_dynamic-slice_fusion.4
  257.2 1.1 constant_dynamic-slice_fusion.4
  273.7 1.1 constant_dynamic-slice_fusion.4
  276.1 1.1 constant_dynamic-slice_fusion.4
  278.4 1.1 constant_dynamic-slice_fusion.4
  309.6 1.2 convolution_bitcast_fusion.7
  310.8 1.5 convolution_bitcast_fusion.6
  313.5 5.3 %convolution_bitcast_fusion = f32[2048,1280]{0,1:T(8,128)} fusion(bf16[1,128,2048]{2,1,0:T(8,128)(2,1)S(1)} %copy-done, bf16[128,128]{0,1:T(8,128)(2,1)S(1)} %fusion.12, bf16[128,128]{0,1:T(8,128)(2,1)S(1)} %fusion.11, bf16[128,1024]{0,1:T(8,128)(2,1)S(1)} %bitcast.132), kind=kOutput, calls=%fused_computation.8 | convolution fusion | flops 672071680 | bytes 11337728 | tf_op jit(solution)/shard_map/dot_general | solution.py:153
  318.9 11.3 %copy.89 = f32[2048,1280]{1,0:T(8,128)} copy(f32[2048,1280]{0,1:T(8,128)} %convolution_bitcast_fusion) | data formatting | bytes 20971520
  330.2 106.7 %reduce-scatter.4.cloned.1.call-done = f32[64,1280]{1,0:T(8,128)} async-done(((f32[2048,1280]{1,0:T(8,128)}), f32[64,1280]{1,0:T(8,128)}) %reduce-scatter.4.cloned.1.call-update) | async-done | bytes 327696
  436.9 2.1 copy.90
  439.0 4.3 convolution_bitcast_fusion.1
  443.4 69.7 %all-reduce.2.cloned.1.call-done = f32[64,1280]{0,1:T(8,128)} async-done(((f32[64,1280]{0,1:T(8,128)}), f32[64,1280]{0,1:T(8,128)}) %all-reduce.2.cloned.1.call-update) | async-done | bytes 327696 | tf_op jit(solution)/shard_map/psum | solution.py:160
  513.0 1.1 broadcast_multiply_fusion
  (170 shorter events, 72.5 us)
Async XLA Ops:
  7.2 72.8 %copy-start = (bf16[1,128,2048]{2,1,0:T(8,128)(2,1)S(1)}, bf16[1,128,2048]{2,1,0:T(8,128)(2,1)}, u32[]{:S(2)}) copy-start(bf16[1,128,2048]{2,1,0:T(8,128)(2,1)} %param.9) | copy-start | bytes 1572868
  7.2 58.5 %all-gather.6.cloned.1.call-start = ((), (), s32[]{:S(2)}) async-start(), calls=%async_computation.1 | async-start | bytes 5406720 | tf_op jit(solution)/shard_map/all_gather | solution.py:108
  7.9 152.9 %all-gather.10.cloned.1.call-start = ((), (), s32[]{:S(2)}) async-start(), calls=%async_computation.3 | async-start | bytes 17301504 | tf_op jit(solution)/shard_map/all_gather | solution.py:12
  77.6 2.4 copy-start.2
  79.9 3.4 copy-start.5
  83.3 157.1 %all-gather.8.cloned.1.call-start = ((), (), s32[]{:S(2)}) async-start(), calls=%async_computation.2 | async-start | bytes 17301504 | tf_op jit(solution)/shard_map/all_gather | solution.py:12
  83.6 77.2 %copy-start.3 = (bf16[1,128,1024]{1,2,0:T(8,128)(2,1)}, bf16[1,128,1024]{1,2,0:T(8,128)(2,1)S(1)}, u32[]{:S(2)}) copy-start(bf16[1,128,1024]{1,2,0:T(8,128)(2,1)S(1)} %copy.63) | copy-start | bytes 786436
  85.4 351.5 %reduce-scatter.4.cloned.1.call-start = ((), (), s32[]{:S(2)}) async-start(), calls=%async_computation.5 | async-start | bytes 10813440
  106.9 53.9 %copy-start.7 = (pred[128,128]{0,1:T(8,128)(4,1)}, pred[128,128]{0,1:T(8,128)(4,1)S(1)}, u32[]{:S(2)}) copy-start(pred[128,128]{0,1:T(8,128)(4,1)S(1)} %iota_compare_fusion) | copy-start | bytes 49156
  165.6 74.9 %copy-start.1 = (f32[16,128,64]{2,1,0:T(8,128)}, f32[16,128,64]{2,1,0:T(8,128)S(1)}, u32[]{:S(2)}) copy-start(f32[16,128,64]{2,1,0:T(8,128)S(1)} %get-tuple-element.218) | copy-start | bytes 1572868
  309.2 3.7 copy-start.4
  309.2 3.7 copy-start.6
  309.2 3.7 copy-start.8
  309.3 3.7 copy-start.9
  330.2 182.8 %all-reduce.2.cloned.1.call-start = ((), (), s32[]{:S(2)}) async-start(), calls=%async_computation.4 | async-start | bytes 1310720 | tf_op jit(solution)/shard_map/psum | solution.py:160
Sparse Core Ops, SparseCore 0:
  10.6 55.0 all-gather.5
  83.4 77.2 all-gather.9
  163.3 77.0 all-gather.7
  330.3 106.5 reduce-scatter.3
  439.2 73.7 all-reduce.1
where the time goes:
time: 525 us; the launch traced here: 522 us
  waiting for transfers between devices  333 us (63%)
  local copies, waits for them, and re-layouts  91.1 us (17%)
  blocking collectives  46 us (9%)
  matrix products  18.9 us (4%)
  other arithmetic  17.6 us (3%)
  between operations  14 us (3%)
    all_gather x2, waiting for transfers between devices, entering(): gathered = jax.tree.map(lambda a: lax.all_gather(a, axis), part)  127 us
    unnamed x6, waiting for transfers between devices  107 us
    psum x1, waiting for transfers between devices, local(): summed_grad = lax.psum(partial_grad, 'dp')  69.7 us
    dynamic_slice x62, local copies, waits for them, and re-layouts, one(): lax.dynamic_index_in_dim(a, source, 0, False)  43.9 us
    all_gather x1, waiting for transfers between devices, local(): lax.all_gather(weight_codes, 'seq', axis=0, tiled=True)  28.6 us
    all_gather x1, blocking collectives, local(): lax.all_gather(scales, 'seq', axis=0, tiled=True)  24.6 us
    mul x31, local copies, waits for them, and re-layouts, join_summary(): later[0][:, None, None] * earlier[1] + later[1]  21.4 us
    all_gather x1, blocking collectives, entering(): gathered = jax.tree.map(lambda a: lax.all_gather(a, axis), part)  21.4 us
  transfers between devices with their start and end apart: 5, of which 5 were waited for; matrix products, arithmetic and copies ran while one was open for 3% of the time, Pallas kernels for 0%

commit v1 on v0

--- a/solution.py
+++ b/solution.py
@@ -3,6 +3,11 @@
 import jax.numpy as jnp
 from jax import lax
 from jax.sharding import PartitionSpec as P
+
+
+def exchange_gather(x, name, along):
+    outgoing = jnp.stack([x] * lax.axis_size(name))
+    return jnp.concatenate(lax.all_to_all(outgoing, name, 0, 0), axis=along)
 
 
 def entering(part, axis, combine, identity, reverse):
@@ -105,7 +110,7 @@
     proj_width = weight_codes.shape[1]
     state_width = (proj_width - hp_width) // 2
     full_codes, full_scales = (
-        lax.all_gather(weight_codes, "seq", axis=0, tiled=True),
+        exchange_gather(weight_codes, "seq", 0),
         lax.all_gather(scales, "seq", axis=0, tiled=True),
     )
     weights = dequantize(full_codes, full_scales)

time: 525 us -> 590 us (1.12)
  waiting for transfers between devices: 333 us -> 276 us
  blocking collectives: 46 us -> 98.9 us
  local copies, waits for them, and re-layouts: 91.1 us -> 128 us
  other arithmetic: 17.6 us -> 34.5 us
  starting transfers between devices: 0.2 us -> 7.84 us
  matrix products: 18.9 us -> 25.4 us
    all_gather x2, waiting for transfers between devices: 127 us -> 61.2 us  [entering(): gathered = jax.tree.map(lambda a: lax.all_gather(a, axis), part)]
    all_gather x1, blocking collectives: 24.6 us -> 76.3 us  [local(): lax.all_gather(scales, 'seq', axis=0, tiled=True)]
    unnamed x6 -> x5, waiting for transfers between devices: 107 us -> 146 us
    all_gather x1 -> x0, waiting for transfers between devices: 28.6 us -> none  [local(): lax.all_gather(weight_codes, 'seq', axis=0, tiled=True)]
    convert_element_type x0 -> x2, local copies, waits for them, and re-layouts: none -> 23.8 us  [the longest x1 11.9 us: dequantize(): code_rows.astype(jnp.float32)]
    convert_element_type x1 -> x2, other arithmetic: 3.92 us -> 23.6 us  [dequantize(): return spread.reshape(row_count, col_count).astype(jnp.bfloat16)]
    mul x0 -> x2, local copies, waits for them, and re-layouts: none -> 16.5 us  [dequantize(): spread = spread * scale_rows.astype(jnp.float32)[:, :, None]]
    all_gather x1 -> x0, local copies, waits for them, and re-layouts: 7.95 us -> none  [local(): lax.all_gather(weight_codes, 'seq', axis=0, tiled=True)]
  transfers between devices with their start and end apart: 5 -> 5, of which waited for: 5 -> 4; matrix products, arithmetic and copies ran while one was open for 3% -> 19% of each run, Pallas kernels for 0% -> 0%
where the time goes in v1:
time: 590 us; the launch traced here: 586 us
  waiting for transfers between devices  276 us (47%)
  local copies, waits for them, and re-layouts  128 us (22%)
  blocking collectives  98.9 us (17%)
  other arithmetic  34.5 us (6%)
  matrix products  25.4 us (4%)
  between operations  14 us (2%)
  starting transfers between devices  7.84 us (1%)
    unnamed x5, waiting for transfers between devices  146 us
    all_gather x1, blocking collectives, local(): lax.all_gather(scales, 'seq', axis=0, tiled=True)  76.3 us
    psum x1, waiting for transfers between devices, local(): summed_grad = lax.psum(partial_grad, 'dp')  68.7 us
    all_gather x2, waiting for transfers between devices, entering(): gathered = jax.tree.map(lambda a: lax.all_gather(a, axis), part)  61.2 us
    dynamic_slice x62, local copies, waits for them, and re-layouts, one(): lax.dynamic_index_in_dim(a, source, 0, False)  44.4 us
    convert_element_type x2, other arithmetic, dequantize(): return spread.reshape(row_count, col_count).astype(jnp.bfloat16)  23.6 us
    all_gather x1, blocking collectives, entering(): gathered = jax.tree.map(lambda a: lax.all_gather(a, axis), part)  22.6 us
    mul x31, local copies, waits for them, and re-layouts, join_summary(): later[0][:, None, None] * earlier[1] + later[1]  21.3 us
  transfers between devices with their start and end apart: 5, of which 4 were waited for; matrix products, arithmetic and copies ran while one was open for 19% of the time, Pallas kernels for 0%

profile of v1, /device:TPU:2, one launch (start us, length us, event | category | flops | bytes accessed | tf_op | source)
XLA Modules:
  0.0 586.0 jit_solution(12791751854829433891)
XLA Ops:
  7.2 3.9 stack.2
  11.1 7.7 %all-to-all-start = ((bf16[32,64,1280]{2,1,0:T(8,128)(2,1)}), bf16[32,64,1280]{2,1,0:T(8,128)(2,1)}, u32[]{:S(2)}, u32[]{:S(2)}) async-start(bf16[32,64,1280]{2,1,0:T(8,128)(2,1)} %stack.2), calls=%async_computation | async-start | bytes 10485760 | tf_op jit(solution)/shard_map/all_to_all | solution.py:10
  19.5 76.3 %all-gather.1 = bf16[32,64,10]{1,2,0:T(8,128)(2,1)S(1)} all-gather(bf16[1,64,10]{1,2,0:T(8,128)(2,1)S(1)} %bitcast.150), channel_id=1, replica_groups=mesh['dp'=8,'seq'=32] {'seq'}, dimensions={0}, use_global_device_ids=true | all-gather | bytes 42240 | tf_op jit(solution)/shard_map/all_gather | solution.py:114
  98.2 11.9 %reshape.199 = f32[2048,10,128]{2,1,0:T(8,128)} reshape(bf16[32,64,1280]{2,1,0:T(8,128)(2,1)} %all-to-all-done) | data formatting | bytes 15728640 | tf_op jit(solution)/shard_map/convert_element_type | solution.py:32
  110.1 14.6 %multiply_convert_fusion = bf16[2048,10,128]{2,1,0:T(8,128)(2,1)} fusion(f32[2048,10,128]{2,1,0:T(8,128)} %reshape.199, f32[2048,10]{1,0:T(8,128)S(1)} %bitcast.134), kind=kLoop, calls=%fused_computation.6 | loop fusion | flops 5242880 | bytes 15810560 | tf_op jit(solution)/shard_map/convert_element_type | solution.py:34
  124.7 11.9 %copy.88 = bf16[2048,10,128]{0,2,1:T(8,128)(2,1)} copy(bf16[2048,10,128]{2,1,0:T(8,128)(2,1)} %multiply_convert_fusion) | data formatting | bytes 10485760 | tf_op jit(solution)/shard_map/convert_element_type | solution.py:34
  136.6 4.0 fusion.1
  143.6 22.6 %all-gather = f32[32,16,1]{1,2,0:T(1,128)} all-gather(f32[1,16,1]{1,2,0:T(1,128)S(1)} %exp.58), channel_id=2, replica_groups=mesh['dp'=8,'seq'=32] {'seq'}, dimensions={0}, use_global_device_ids=true | all-gather | bytes 2112 | tf_op jit(solution)/shard_map/all_gather | solution.py:17
  168.1 53.7 %all-gather.5.cloned.1.call-done = f32[32,16,128,64]{2,3,1,0:T(8,128)} async-done(((f32[1,16,128,64]{2,3,1,0:T(8,128)}), f32[32,16,128,64]{2,3,1,0:T(8,128)}) %all-gather.5.cloned.1.call-update) | async-done | bytes 16777232 | tf_op jit(solution)/shard_map/all_gather | solution.py:17
  221.9 69.2 %while.16 = (s32[]{:T(128)}, f32[16,128,64]{2,1,0:T(8,128)S(1)}, s32[]{:T(128)}, f32[32,16]{1,0:T(8,128)}, f32[32,16,128,64]{2,3,1,0:T(8,128)}, /*index=5*/s32[]{:T(128)}, s32[]{:T(128)}, s32[]{:T(128)}, s32[]{:T(128)}) while((s32[]{:T(128)}, f32[16,128,64]{2,1,0:T(8,128)S(1)}, s32[]{:T(128)}, f32[32,16]{1,0:T(8,128)}, ...), condition=%wide.region_2.3_spmd, body=%wide.region_1.2_spmd.sunk | while | flops 262150 | bytes 3670355 | solution.py:26
  236.1 1.1 constant_dynamic-slice_fusion.4
  262.3 1.2 constant_dynamic-slice_fusion.4
  272.0 1.2 constant_dynamic-slice_fusion.4
  283.9 1.1 constant_dynamic-slice_fusion.4
  288.7 1.2 constant_dynamic-slice_fusion.4
  292.1 1.9 convolution_bitcast_fusion.7
  294.0 7.5 %all-gather.7.cloned.1.call-done = f32[32,16,128,64]{2,3,1,0:T(8,128)} async-done(((f32[1,16,128,64]{2,3,1,0:T(8,128)}), f32[32,16,128,64]{2,3,1,0:T(8,128)}) %all-gather.7.cloned.1.call-update) | async-done | bytes 16777232 | tf_op jit(solution)/shard_map/all_gather | solution.py:17
  301.6 4.9 while.17
  307.5 1.2 convolution_bitcast_fusion.6
  308.9 1.2 fusion.32
  310.0 1.6 fusion.10
  311.6 5.3 convolution_bitcast_fusion
  317.0 11.3 %copy.120 = f32[2048,1280]{1,0:T(8,128)} copy(f32[2048,1280]{0,1:T(8,128)} %convolution_bitcast_fusion) | data formatting | bytes 20971520
  328.3 1.1 copy-done.2
  329.8 5.3 mul.263.clone
  335.1 11.2 %copy.106 = f32[2048,1280]{1,0:T(8,128)} copy(f32[2048,1280]{0,1:T(8,128)} %bitcast.133) | data formatting | bytes 20971520 | tf_op jit(solution)/shard_map/mul | solution.py:33
  346.3 9.0 %fusion = bf16[2048,1280]{1,0:T(8,128)(2,1)} fusion(f32[2048,1280]{1,0:T(8,128)} %copy.106, bf16[32,64,1280]{2,1,0:T(8,128)(2,1)} %all-to-all-done), kind=kLoop, calls=%fused_computation.8 | loop fusion | flops 7864320 | bytes 20971520 | tf_op jit(solution)/shard_map/convert_element_type | solution.py:34
  355.3 146.0 %reduce-scatter.4.cloned.1.call-done = f32[64,1280]{1,0:T(8,128)} async-done(((f32[2048,1280]{1,0:T(8,128)}), f32[64,1280]{1,0:T(8,128)}) %reduce-scatter.4.cloned.1.call-update) | async-done | bytes 327696
  501.2 2.1 copy.121
  503.3 5.3 convolution_bitcast_fusion.1
  508.6 68.7 %all-reduce.2.cloned.1.call-done = f32[64,1280]{0,1:T(8,128)} async-done(((f32[64,1280]{0,1:T(8,128)}), f32[64,1280]{0,1:T(8,128)}) %all-reduce.2.cloned.1.call-update) | async-done | bytes 327696 | tf_op jit(solution)/shard_map/psum | solution.py:165
  577.3 1.1 broadcast_multiply_fusion
  (171 shorter events, 78.1 us)
Async XLA Ops:
  7.2 129.4 %copy-start = (bf16[1,128,2048]{2,1,0:T(8,128)(2,1)S(1)}, bf16[1,128,2048]{2,1,0:T(8,128)(2,1)}, u32[]{:S(2)}) copy-start(bf16[1,128,2048]{2,1,0:T(8,128)(2,1)} %param.9) | copy-start | bytes 1572868
  7.2 11.6 %copy-start.5 = (f32[1,16,128]{2,1,0:T(8,128)S(1)}, f32[1,16,128]{2,1,0:T(8,128)}, u32[]{:S(2)}) copy-start(f32[1,16,128]{2,1,0:T(8,128)} %param.12) | copy-start | bytes 24580
  7.2 12.1 %copy-start.4 = (bf16[1,128,1024]{2,1,0:T(8,128)(2,1)S(1)}, bf16[1,128,1024]{2,1,0:T(8,128)(2,1)}, u32[]{:S(2)}) copy-start(bf16[1,128,1024]{2,1,0:T(8,128)(2,1)} %param.13) | copy-start | bytes 786436
  7.2 12.2 %copy-start.7 = (bf16[64,10]{0,1:T(8,128)(2,1)S(1)}, bf16[64,10]{0,1:T(8,128)(2,1)}, u32[]{:S(2)}) copy-start(bf16[64,10]{0,1:T(8,128)(2,1)} %param.11) | copy-start | bytes 3844
  11.1 87.1 %all-to-all-start = ((bf16[32,64,1280]{2,1,0:T(8,128)(2,1)}), bf16[32,64,1280]{2,1,0:T(8,128)(2,1)}, u32[]{:S(2)}, u32[]{:S(2)}) async-start(bf16[32,64,1280]{2,1,0:T(8,128)(2,1)} %stack.2), calls=%async_computation | async-start | bytes 10485760 | tf_op jit(solution)/shard_map/all_to_all | solution.py:10
  18.8 203.1 %all-gather.5.cloned.1.call-start = ((), (), s32[]{:S(2)}) async-start(), calls=%async_computation.2 | async-start | bytes 17301504 | tf_op jit(solution)/shard_map/all_gather | solution.py:17
  19.4 146.9 %copy-start.3 = (bf16[1,128,1024]{1,2,0:T(8,128)(2,1)}, bf16[1,128,1024]{1,2,0:T(8,128)(2,1)S(1)}, u32[]{:S(2)}) copy-start(bf16[1,128,1024]{1,2,0:T(8,128)(2,1)S(1)} %copy.91) | copy-start | bytes 786436
  96.2 13.9 %copy-start.1 = (f32[32,64,10]{2,1,0:T(8,128)}, f32[32,64,10]{2,1,0:T(8,128)S(1)}, u32[]{:S(2)}) copy-start(f32[32,64,10]{2,1,0:T(8,128)S(1)} %copy.115) | copy-start | bytes 245764
  141.7 159.8 %all-gather.7.cloned.1.call-start = ((), (), s32[]{:S(2)}) async-start(), calls=%async_computation.3 | async-start | bytes 17301504 | tf_op jit(solution)/shard_map/all_gather | solution.py:17
  143.6 357.7 %reduce-scatter.4.cloned.1.call-start = ((), (), s32[]{:S(2)}) async-start(), calls=%async_computation.5 | async-start | bytes 10813440
  166.3 55.6 %copy-start.6 = (pred[128,128]{0,1:T(8,128)(4,1)}, pred[128,128]{0,1:T(8,128)(4,1)S(1)}, u32[]{:S(2)}) copy-start(pred[128,128]{0,1:T(8,128)(4,1)S(1)} %iota_compare_fusion) | copy-start | bytes 49156
  328.2 1.2 copy-start.2
  328.3 249.1 %all-reduce.2.cloned.1.call-start = ((), (), s32[]{:S(2)}) async-start(), calls=%async_computation.4 | async-start | bytes 1310720 | tf_op jit(solution)/shard_map/psum | solution.py:165
Sparse Core Ops, SparseCore 0:
  141.8 79.9 all-gather.4
  224.4 77.0 all-gather.6
  328.4 172.8 reduce-scatter.3
  503.6 73.7 all-reduce.1
